TPU v7x, 32 devices: a whole 2x2x4 slice. The times are simulated.
32 devices in a mesh: section: 2 (over core), fsdp: 2 (over y), expert: 8 (over z, x).
Axes of the slice: x: 2, y: 2, z: 4, core: 2. Of those that a mesh axis runs over, the one named last changes fastest.
Arguments:
- tokens: bfloat16 [2048, 2048], P(('fsdp', 'expert')), may hold values from -40 to 40
- norm_gain: float32 [2, 2048], P('section'), may hold values from 0.5 to 1.5
- router: bfloat16 [2, 2048, 32], P('section'), may hold values from -0.3125 to 0.3125
- w_gate: bfloat16 [2, 32, 2048, 768], P('section', 'expert', 'fsdp'), may hold values from -0.125 to 0.125
- w_up: bfloat16 [2, 32, 2048, 768], P('section', 'expert', 'fsdp'), may hold values from -0.125 to 0.125
- w_down: bfloat16 [2, 32, 768, 2048], P('section', 'expert', None, 'fsdp'), may hold values from -0.21875 to 0.21875
- routes: int32 [2, 2048, 6], P('section', ('fsdp', 'expert')), may hold values from 0 to 31, all different within a row; in each aligned block of 64 rows (0 to 63, 64 to 127, ..., all dimensions but the last counted through in order) at most 14 rows name the same one
Outputs:
- final_out: bfloat16 [2048, 2048], P(('fsdp', 'expert'), 'section')
- layer_stats: float32 [2], P('section')
Inputs may be any that keep to these rules, and one draw needn't show every extreme that they name: `routes`: each row names 6 different experts; in every aligned block of 64 rows of one layer no expert is named by more than 14 rows, a bound that some block reaches.
All inputs are finite; a program needn't handle non-finite values.
Results may differ from a plain program's by a relative error of at most 0.0065.
Values may be sent and summed in bfloat16 or wider, within the bound.
No kernel may reach another device: no remote copies, remote signals or barrier semaphores. Data moves between devices by JAX's collectives and lax.ppermute only.
A program may use at most 192 MiB of HBM per device.

v0:
```python
import jax
import jax.numpy as jnp
from jax import lax
from jax.sharding import PartitionSpec as P

TOP = 6
BLOCK = 64
epsilon = 1e-06


def other_section(value):
    return lax.ppermute(value, "section", [(0, 1), (1, 0)])


def ring_pairs(count, shift):
    return [(source, (source + shift) % count) for source in range(count)]


def rms_scaled(hidden_rows, gain_row):
    values = hidden_rows.astype(jnp.float32)
    scale = lax.rsqrt(jnp.mean(values * values, axis=-1, keepdims=True) + epsilon)
    return (values * scale * gain_row).astype(jnp.bfloat16)


def gate_weights(normed, router_weight, route_rows):
    logits = jnp.dot(normed, router_weight, preferred_element_type=jnp.float32)
    scores = jax.nn.sigmoid(logits)
    expert_ids = jnp.arange(router_weight.shape[1], dtype=jnp.int32)
    chosen_mask = (route_rows[:, :, None] == expert_ids[None, None, :]).astype(jnp.float32)
    chosen = jnp.sum(scores[:, None, :] * chosen_mask, axis=2)
    return chosen / jnp.sum(chosen, axis=1, keepdims=True)


def slot_positions(route_rows, experts_count, capacity):
    flat_routes = route_rows.reshape(-1)
    onehot = (flat_routes[:, None] == jnp.arange(experts_count, dtype=jnp.int32)[None, :]).astype(
        jnp.int32
    )
    count = flat_routes.shape[0]
    earlier = (jnp.arange(count)[:, None] > jnp.arange(count)[None, :]).astype(jnp.bfloat16)
    before = jnp.dot(
        earlier, onehot.astype(jnp.bfloat16), preferred_element_type=jnp.float32
    ).astype(jnp.int32)
    slot_index = jnp.sum(before * onehot, axis=1)
    return (flat_routes * capacity + slot_index).reshape(route_rows.shape)


def other_half(value):
    return lax.ppermute(value, "zhalf", [(0, 1), (1, 0)])


def half_buffer(positions, normed, slot_ids, fsdp_count, chunk):
    placing = jnp.any(positions[:, :, None] == slot_ids[None, None, :], axis=1).astype(jnp.bfloat16)
    return jnp.einsum(
        "rs,rfd->fsd",
        placing,
        normed.reshape(normed.shape[0], fsdp_count, chunk),
        preferred_element_type=jnp.float32,
    ).astype(jnp.bfloat16)


def expert_layer(entering, route_rows, partner_routes, gain_row, router_weight, weights, capacity):
    gate_w, up_w, down_w = weights
    rows, width = entering.shape
    experts_count = router_weight.shape[1]
    local_experts, chunk, hidden_units = gate_w.shape
    fsdp_count = lax.axis_size("fsdp")
    halves = lax.axis_size("zhalf")
    inner_devices = lax.axis_size("inner")
    half_index = lax.axis_index("zhalf")
    fsdp_index = lax.axis_index("fsdp")
    partner_entering = other_half(entering)
    normed = rms_scaled(entering, gain_row)
    partner_normed = rms_scaled(partner_entering, gain_row)
    mix_weights = gate_weights(normed, router_weight, route_rows)
    positions = slot_positions(route_rows, experts_count, capacity)
    partner_positions = slot_positions(partner_routes, experts_count, capacity)
    half_slots = experts_count // halves * capacity
    local_ids = half_index * half_slots + jnp.arange(half_slots, dtype=jnp.int32)
    first_half = half_index == 0
    lower_normed = jnp.where(first_half, normed, partner_normed)
    upper_normed = jnp.where(first_half, partner_normed, normed)
    lower_positions = jnp.where(first_half, positions, partner_positions)
    upper_positions = jnp.where(first_half, partner_positions, positions)
    group_slots = local_experts * capacity
    both_positions = jnp.stack([lower_positions, upper_positions])
    placing = jnp.any(
        both_positions[:, :, :, None] == local_ids[None, None, None, :], axis=2
    ).astype(jnp.bfloat16)
    placing = placing.reshape(halves, rows, inner_devices, local_experts, capacity)
    both_normed = jnp.stack([lower_normed, upper_normed]).reshape(halves, rows, fsdp_count, chunk)
    outgoing = (
        jnp.einsum("prijc,prfd->fijpcd", placing, both_normed, preferred_element_type=jnp.float32)
        .astype(jnp.bfloat16)
        .reshape(fsdp_count * inner_devices, local_experts, halves * capacity, chunk)
    )
    arrived = lax.all_to_all(outgoing, ("fsdp", "inner"), 0, 2, tiled=True)
    sources = fsdp_count * inner_devices * halves
    arrived_blocks = arrived.reshape(local_experts, fsdp_count, -1, chunk)

    def gate_and_up(rows_in):
        gate_part = jnp.einsum("jrd,jdh->jrh", rows_in, gate_w, preferred_element_type=jnp.float32)
        up_part = jnp.einsum("jrd,jdh->jrh", rows_in, up_w, preferred_element_type=jnp.float32)
        return (gate_part, up_part)

    received = []
    for shift in range(1, fsdp_count):
        target = (fsdp_index + shift) % fsdp_count
        outgoing_pair = jnp.stack(
            gate_and_up(lax.dynamic_index_in_dim(arrived_blocks, target, 1, keepdims=False))
        ).astype(jnp.bfloat16)
        received.append(lax.ppermute(outgoing_pair, "fsdp", ring_pairs(fsdp_count, shift)))
    gate_sum, up_sum = gate_and_up(
        lax.dynamic_index_in_dim(arrived_blocks, fsdp_index, 1, keepdims=False)
    )
    for got in received:
        gate_sum = gate_sum + got[0].astype(jnp.float32)
        up_sum = up_sum + got[1].astype(jnp.float32)
    inner_act = (jax.nn.silu(gate_sum) * up_sum).astype(jnp.bfloat16)
    inner_pieces = [inner_act]
    for shift in range(1, fsdp_count):
        inner_pieces.append(lax.ppermute(inner_act, "fsdp", ring_pairs(fsdp_count, shift)))
    order = (fsdp_index - jnp.arange(fsdp_count, dtype=jnp.int32)) % fsdp_count
    inner_all = jnp.take(jnp.stack(inner_pieces), order, axis=0).reshape(
        fsdp_count, local_experts, inner_devices, halves, capacity, hidden_units
    )
    sending = jnp.einsum(
        "fjipch,jhd->fpijcd", inner_all, down_w, preferred_element_type=jnp.float32
    ).astype(jnp.bfloat16)
    returned = lax.all_to_all(
        sending.reshape(sources, group_slots, chunk), ("fsdp", "zhalf", "inner"), 0, 0, tiled=True
    )
    slot_ids = jnp.arange(experts_count * capacity, dtype=jnp.int32)
    hits = positions[:, :, None] == slot_ids[None, None, :]
    combining = jnp.sum(jnp.where(hits, mix_weights[:, :, None], 0.0), axis=1)
    branch_sum = jnp.einsum(
        "rs,fsd->rfd",
        combining,
        returned.reshape(fsdp_count, experts_count * capacity, chunk).astype(jnp.float32),
        precision=lax.Precision.HIGHEST,
        preferred_element_type=jnp.float32,
    ).reshape(rows, width)
    return (entering.astype(jnp.float32) + branch_sum).astype(jnp.bfloat16)


def body(tokens, norm_gain, router, w_gate, w_up, w_down, routes):
    section_index = lax.axis_index("section")
    sections = lax.axis_size("section")
    token_rows, width = tokens.shape
    piece = token_rows // sections
    experts_count = router.shape[2]
    block_capacity = (7 * BLOCK * TOP + 6 * experts_count - 1) // (6 * experts_count)
    capacity = block_capacity * (piece // BLOCK)
    own_weights = (w_gate[0], w_up[0], w_down[0])
    other_weights = tuple((other_section(w) for w in own_weights))
    own_small = (norm_gain[0], router[0])
    packed = jnp.concatenate([own_small[0][:, None], own_small[1].astype(jnp.float32)], axis=1)
    other_packed = other_section(packed)
    other_small = (other_packed[:, 0], other_packed[:, 1:].astype(router.dtype))
    own_routes = routes[0]
    section_routes = other_section(own_routes)
    half_routes = other_half(own_routes)
    diagonal_routes = lax.ppermute(
        own_routes, ("section", "zhalf"), [(0, 3), (3, 0), (1, 2), (2, 1)]
    )
    hidden = lax.dynamic_slice_in_dim(tokens, section_index * piece, piece, 0)
    squares = []
    for layer in range(sections):
        mine = section_index == layer
        gain_row, router_weight = [jnp.where(mine, a, b) for a, b in zip(own_small, other_small)]
        weights = tuple((jnp.where(mine, a, b) for a, b in zip(own_weights, other_weights)))
        route_all = jnp.where(mine, own_routes, section_routes)
        partner_all = jnp.where(mine, half_routes, diagonal_routes)
        route_rows = lax.dynamic_slice_in_dim(route_all, section_index * piece, piece, 0)
        partner_rows = lax.dynamic_slice_in_dim(partner_all, section_index * piece, piece, 0)
        hidden = expert_layer(
            hidden, route_rows, partner_rows, gain_row, router_weight, weights, capacity
        )
        values = hidden.astype(jnp.float32)
        squares.append(jnp.sum(values * values))
    everyone = ("section", "fsdp", "zhalf", "inner")
    expert_devices = lax.axis_size("zhalf") * lax.axis_size("inner")
    device_count = sections * lax.axis_size("fsdp") * expert_devices
    square_rows = jnp.broadcast_to(jnp.stack(squares)[None, :], (device_count, sections))
    totals = jnp.sum(lax.all_to_all(square_rows, everyone, 0, 0, tiled=True), axis=0)
    token_total = token_rows * lax.axis_size("fsdp") * expert_devices
    stats = jnp.sqrt(totals / (token_total * width))
    layer_stats = lax.dynamic_slice_in_dim(stats, section_index, 1, 0)
    half_width = width // 2
    keep = lax.dynamic_slice_in_dim(hidden, section_index * half_width, half_width, 1)
    send = lax.dynamic_slice_in_dim(hidden, (1 - section_index) * half_width, half_width, 1)
    arrived = other_section(send)
    final_out = jnp.where(
        section_index == 0,
        jnp.concatenate([keep, arrived], axis=0),
        jnp.concatenate([arrived, keep], axis=0),
    )
    return (final_out, layer_stats)


def solution(mesh):
    sizes = dict(zip(mesh.axis_names, mesh.devices.shape))
    devices = mesh.devices.reshape(sizes["section"], sizes["fsdp"], 2, sizes["expert"] // 2)
    split_mesh = jax.sharding.Mesh(devices, ("section", "fsdp", "zhalf", "inner"))
    tokens_axes = ("fsdp", "zhalf", "inner")
    experts_axes = ("zhalf", "inner")
    in_specs = (
        P(tokens_axes, None),
        P("section", None),
        P("section", None, None),
        P("section", experts_axes, "fsdp", None),
        P("section", experts_axes, "fsdp", None),
        P("section", experts_axes, None, "fsdp"),
        P("section", tokens_axes, None),
    )
    out_specs = (P(tokens_axes, "section"), P("section"))
    return jax.shard_map(
        body, mesh=split_mesh, in_specs=in_specs, out_specs=out_specs, check_vma=False
    )
```

profile of v0, /device:TPU:0, one launch (start us, length us, event | category | flops | bytes accessed | tf_op | source)
XLA Modules:
  0.0 329.2 jit_solution(16897650569379515647)
XLA Ops:
  0.6 0.8 copy.121
  1.4 4.1 %collective-permute-start.4 = (s32[128,6]{1,0:T(8,128)S(1)}, s32[128,6]{1,0:T(8,128)S(1)}, u32[]{:S(2)}, u32[]{:S(2)}) collective-permute-start(s32[128,6]{1,0:T(8,128)S(1)} %bitcast.209), channel_id=1, source_target_pairs={{0,4},{4,0},{1,5},{5,1},{2,6},{6,2},{3,7},{7,3},{8,12},{12,8},{9,1... | collective-permute-start | bytes 9224 | tf_op jit(solution)/shard_map/ppermute | solution.py:49
  5.7 1.1 fusion.78
  6.8 2.9 collective-permute-start.3
  9.8 0.9 bitcast_convert_fusion
  10.7 0.8 pad_maximum_fusion.4
  11.6 0.5 collective-permute-start.6
  12.1 5.7 %collective-permute-done.5 = s32[128,6]{1,0:T(8,128)S(1)} collective-permute-done((s32[128,6]{1,0:T(8,128)S(1)}, s32[128,6]{1,0:T(8,128)S(1)}, u32[]{:S(2)}, u32[]{:S(2)}) %collective-permute-start.5) | collective-permute-done | bytes 3104 | tf_op jit(solution)/shard_map/ppermute | solution.py:163
  18.0 0.2 fusion.41
  18.4 0.2 fusion.43
  20.2 0.3 compare_reduce_fusion
  20.7 2.3 collective-permute-done.3
  23.2 0.2 broadcast_select_fusion.45
  23.9 0.7 convert_bitcast_fusion.3
  24.6 2.8 copy.128
  27.4 4.1 %all-to-all-start = ((bf16[8,4,28,1024]{3,1,2,0:T(4,128)(2,1)}), bf16[8,4,28,1024]{3,1,2,0:T(4,128)(2,1)S(1)}, u32[]{:S(2)}, u32[]{:S(2)}) async-start(bf16[8,4,28,1024]{3,1,2,0:T(4,128)(2,1)} %bitcast.198), calls=%async_computation | async-start | bytes 3670016 | tf_op jit(solution)/shard_map/all_to_all | solution.py:97
  31.6 29.0 %all-to-all-done = bf16[8,4,28,1024]{3,1,2,0:T(4,128)(2,1)S(1)} async-done(((bf16[8,4,28,1024]{3,1,2,0:T(4,128)(2,1)}), bf16[8,4,28,1024]{3,1,2,0:T(4,128)(2,1)S(1)}, u32[]{:S(2)}, u32[]{:S(2)}) %all-to-all-start) | async-done | bytes 1835040 | tf_op jit(solution)/shard_map/all_to_all | solution.py:97
  60.6 0.6 constant_dynamic-slice_fusion.4
  61.2 4.8 %fusion.32 = bf16[1,4,112,768]{3,2,1,0:T(8,128)(2,1)S(1)} fusion(bf16[4,1024,768]{2,1,0:T(8,128)(2,1)} %collective-permute-done.6, pred[]{:T(512)S(6)} %eq.78, bf16[4,1,112,1024]{3,0,2,1:T(4,128)(2,1)S(1)} %get-tuple-element.19, bf16[1,4,1024,768]{3,2,1,0:T(8,128)(2,1)} %param.12), kind=kOutput, calls=%fused_computation.48 | convolution fusion | flops 708132864 | bytes 14188545 | tf_op jit(solution)/shard_map/jrd,jdh->jrh/dot_general | solution.py:102
  66.1 1.8 fusion.33
  68.1 0.6 collective-permute-start.8
  68.7 30.0 %collective-permute-done.8 = bf16[2,4,112,768]{3,2,1,0:T(8,128)(2,1)S(1)} collective-permute-done((bf16[2,4,112,768]{3,2,1,0:T(8,128)(2,1)S(1)}, bf16[2,4,112,768]{3,2,1,0:T(8,128)(2,1)S(1)}, u32[]{:S(2)}, u32[]{:S(2)}) %collective-permute-start.8) | collective-permute-done | bytes 1376288 | tf_op jit(solution)/shard_map/ppermute | solution.py:112
  98.8 1.9 fusion.27
  100.6 2.0 multiply_convert_fusion.1
  102.7 0.6 collective-permute-start.9
  103.4 10.8 %collective-permute-done.9 = bf16[4,112,768]{2,1,0:T(8,128)(2,1)S(1)} collective-permute-done((bf16[4,112,768]{2,1,0:T(8,128)(2,1)S(1)}, bf16[4,112,768]{2,1,0:T(8,128)(2,1)S(1)}, u32[]{:S(2)}, u32[]{:S(2)}) %collective-permute-start.9) | collective-permute-done | bytes 688160 | tf_op jit(solution)/shard_map/ppermute | solution.py:122
  114.3 0.6 gather_fusion
  115.2 0.7 copy.131
  115.9 4.7 %convert_bitcast_fusion.2 = bf16[2,2,4,4,14,1024]{5,4,1,2,0,3:T(8,128)(2,1)S(1)} fusion(bf16[4,768,1024]{2,1,0:T(8,128)(2,1)} %collective-permute-done.2, pred[]{:T(512)S(6)} %eq.78, bf16[2,4,4,2,14,768]{5,1,4,3,2,0:T(4,128)(2,1)S(1)} %bitcast.203, bf16[1,4,768,1024]{3,2,1,0:T(8,128)(2,1)} %param.14), kind=kOutput, calls=%fused_computation.28 | convolution fusion | flops 1413349376 | bytes 15794177 | tf_op jit(solution)/shard_map/fjipch,jhd->fpijcd/dot_general | solution.py:127
  120.8 1.5 reshape.228
  122.3 4.5 %all-to-all-start.1 = ((bf16[16,56,1024]{2,1,0:T(8,128)(2,1)}), bf16[16,56,1024]{2,1,0:T(8,128)(2,1)S(1)}, u32[]{:S(2)}, u32[]{:S(2)}) async-start(bf16[16,56,1024]{2,1,0:T(8,128)(2,1)} %reshape.228), calls=%async_computation.1 | async-start | bytes 3670016 | tf_op jit(solution)/shard_map/all_to_all | solution.py:130
  127.0 0.3 fusion.49
  127.5 39.0 %all-to-all-done.1 = bf16[16,56,1024]{2,1,0:T(8,128)(2,1)S(1)} async-done(((bf16[16,56,1024]{2,1,0:T(8,128)(2,1)}), bf16[16,56,1024]{2,1,0:T(8,128)(2,1)S(1)}, u32[]{:S(2)}, u32[]{:S(2)}) %all-to-all-start.1) | async-done | bytes 1835040 | tf_op jit(solution)/shard_map/all_to_all | solution.py:130
  166.6 1.7 fusion.70
  168.3 2.0 collective-permute-start.10
  170.5 10.9 %collective-permute-done.10 = bf16[64,2048]{1,0:T(8,128)(2,1)S(1)} collective-permute-done((bf16[64,2048]{1,0:T(8,128)(2,1)S(1)}, bf16[64,2048]{1,0:T(8,128)(2,1)S(1)}, u32[]{:S(2)}, u32[]{:S(2)}) %collective-permute-start.10) | collective-permute-done | bytes 262176 | tf_op jit(solution)/shard_map/ppermute | solution.py:49
  181.6 0.2 broadcast_select_fusion.43
  182.4 0.7 convert_bitcast_fusion.1
  183.1 1.6 copy.142
  184.6 28.3 %all_to_all.46 = bf16[8,4,28,1024]{3,1,2,0:T(4,128)(2,1)S(1)} all-to-all(bf16[8,4,28,1024]{3,1,2,0:T(4,128)(2,1)S(1)} %bitcast.202), channel_id=1, replica_groups=mesh['section'=2,'fsdp'=2,'zhalf'=2,'inner'=4] {'fsdp','inner'}, dimensions={0} | all-to-all | bytes 3670016 | tf_op jit(solution)/shard_map/all_to_all | solution.py:97
  212.9 0.6 constant_dynamic-slice_fusion.2
  213.6 4.8 %fusion.34 = bf16[1,4,112,768]{3,2,1,0:T(8,128)(2,1)S(1)} fusion(bf16[4,1024,768]{2,1,0:T(8,128)(2,1)} %collective-permute-done.6, pred[]{:T(512)S(6)} %eq.172, bf16[4,1,112,1024]{3,0,2,1:T(4,128)(2,1)S(1)} %get-tuple-element.17, bf16[1,4,1024,768]{3,2,1,0:T(8,128)(2,1)S(1)} %bitcast.222), kind=kOutput, calls=%fused_computation.50 | convolution fusion | flops 708132864 | bytes 14188545 | tf_op jit(solution)/shard_map/jrd,jdh->jrh/dot_general | solution.py:102
  218.4 4.7 %fusion.35 = bf16[1,4,112,768]{3,2,1,0:T(8,128)(2,1)S(1)} fusion(bf16[4,1024,768]{2,1,0:T(8,128)(2,1)} %collective-permute-done.7, pred[]{:T(512)S(6)} %eq.172, bf16[4,1,112,1024]{3,0,2,1:T(4,128)(2,1)S(1)} %get-tuple-element.17, bf16[1,4,1024,768]{3,2,1,0:T(8,128)(2,1)S(1)} %bitcast.227), kind=kOutput, calls=%fused_computation.51 | convolution fusion | flops 708132864 | bytes 14188545 | tf_op jit(solution)/shard_map/jrd,jdh->jrh/dot_general | solution.py:103
  223.3 0.6 collective-permute-start.11
  223.9 26.6 %collective-permute-done.11 = bf16[2,4,112,768]{3,2,1,0:T(8,128)(2,1)S(1)} collective-permute-done((bf16[2,4,112,768]{3,2,1,0:T(8,128)(2,1)S(1)}, bf16[2,4,112,768]{3,2,1,0:T(8,128)(2,1)S(1)}, u32[]{:S(2)}, u32[]{:S(2)}) %collective-permute-start.11) | collective-permute-done | bytes 1376288 | tf_op jit(solution)/shard_map/ppermute | solution.py:112
  250.5 4.7 %fusion.25 = f32[4,112,768]{2,1,0:T(8,128)S(1)} fusion(bf16[4,1024,768]{2,1,0:T(8,128)(2,1)} %collective-permute-done.6, pred[]{:T(512)S(6)} %eq.172, bf16[4,1,112,1024]{3,0,2,1:T(4,128)(2,1)S(1)} %get-tuple-element.18, bf16[2,4,112,768]{3,2,1,0:T(8,128)(2,1)S(1)} %collective-permute-done.11, bf16[1,4,1024,768]{3,2,1,0:T(8,128)(2,1)S(1)} %bitcast.222), kind=kOutput, calls=%fused_computation.33 | convolution fusion | flops 708476928 | bytes 15564801 | tf_op jit(solution)/shard_map/jrd,jdh->jrh/dot_general | solution.py:102
  255.2 4.9 %multiply_convert_fusion = bf16[4,112,768]{2,1,0:T(8,128)(2,1)S(1)} fusion(f32[4,112,768]{2,1,0:T(8,128)S(1)} %fusion.25, bf16[4,1024,768]{2,1,0:T(8,128)(2,1)} %collective-permute-done.7, pred[]{:T(512)S(6)} %eq.172, bf16[4,1,112,1024]{3,0,2,1:T(4,128)(2,1)S(1)} %get-tuple-element.18, bf16[2,4,112,768]{3,2,1,0:T(8,128)(2,1)S(1)} %collective-permute-done.11, ...), kind=kOutput, calls=%fused_computation.40 | convolution fusion | flops 710541312 | bytes 16252929 | tf_op jit(solution)/shard_map/jrd,jdh->jrh/dot_general | solution.py:103
  260.2 0.6 collective-permute-start.12
  260.8 10.4 %collective-permute-done.12 = bf16[4,112,768]{2,1,0:T(8,128)(2,1)S(1)} collective-permute-done((bf16[4,112,768]{2,1,0:T(8,128)(2,1)S(1)}, bf16[4,112,768]{2,1,0:T(8,128)(2,1)S(1)}, u32[]{:S(2)}, u32[]{:S(2)}) %collective-permute-start.12) | collective-permute-done | bytes 688160 | tf_op jit(solution)/shard_map/ppermute | solution.py:122
  271.3 0.6 gather_fusion.1
  272.1 0.7 copy.145
  272.9 6.5 %convert_bitcast_fusion = bf16[2,2,4,4,14,1024]{5,4,1,2,0,3:T(8,128)(2,1)S(1)} fusion(bf16[4,768,1024]{2,1,0:T(8,128)(2,1)} %collective-permute-done.2, pred[]{:T(512)S(6)} %eq.172, bf16[2,4,4,2,14,768]{5,1,4,3,2,0:T(4,128)(2,1)S(1)} %bitcast.204, bf16[1,4,768,1024]{3,2,1,0:T(8,128)(2,1)} %param.14), kind=kOutput, calls=%fused_computation.26 | convolution fusion | flops 1413349376 | bytes 15794177 | tf_op jit(solution)/shard_map/fjipch,jhd->fpijcd/dot_general | solution.py:127
  279.6 1.5 reshape.230
  281.1 4.3 %all-to-all-start.3 = ((bf16[16,56,1024]{2,1,0:T(8,128)(2,1)}), bf16[16,56,1024]{2,1,0:T(8,128)(2,1)S(1)}, u32[]{:S(2)}, u32[]{:S(2)}) async-start(bf16[16,56,1024]{2,1,0:T(8,128)(2,1)} %reshape.230), calls=%async_computation.3 | async-start | bytes 3670016 | tf_op jit(solution)/shard_map/all_to_all | solution.py:130
  285.6 0.3 fusion.46
  286.2 27.6 %all-to-all-done.3 = bf16[16,56,1024]{2,1,0:T(8,128)(2,1)S(1)} async-done(((bf16[16,56,1024]{2,1,0:T(8,128)(2,1)}), bf16[16,56,1024]{2,1,0:T(8,128)(2,1)S(1)}, u32[]{:S(2)}, u32[]{:S(2)}) %all-to-all-start.3) | async-done | bytes 1835040 | tf_op jit(solution)/shard_map/all_to_all | solution.py:130
  313.9 1.7 multiply_reduce_fusion
  315.6 1.4 pad_maximum_fusion.5
  317.0 0.6 broadcast_in_dim.32
  317.6 3.1 all-to-all-start.4
  320.7 0.3 collective-permute-start.13
  321.1 6.7 %all-to-all-done.4 = f32[32,1,2]{2,1,0:T(1,128)S(1)} async-done(((f32[32,1,2]{2,1,0:T(1,128)}), f32[32,1,2]{2,1,0:T(1,128)S(1)}, u32[]{:S(2)}, u32[]{:S(2)}) %all-to-all-start.4) | async-done | bytes 288 | tf_op jit(solution)/shard_map/all_to_all | solution.py:185
  327.9 0.6 dynamic_slice.48
  328.5 0.8 maximum_select_fusion
  (107 shorter events, 6.2 us)
Async XLA Ops:
  1.4 10.2 %collective-permute-start.4 = (s32[128,6]{1,0:T(8,128)S(1)}, s32[128,6]{1,0:T(8,128)S(1)}, u32[]{:S(2)}, u32[]{:S(2)}) collective-permute-start(s32[128,6]{1,0:T(8,128)S(1)} %bitcast.209), channel_id=1, source_target_pairs={{0,4},{4,0},{1,5},{5,1},{2,6},{6,2},{3,7},{7,3},{8,12},{12,8},{9,1... | collective-permute-start | bytes 9224 | tf_op jit(solution)/shard_map/ppermute | solution.py:49
  5.5 12.3 %collective-permute-start.5 = (s32[128,6]{1,0:T(8,128)S(1)}, s32[128,6]{1,0:T(8,128)S(1)}, u32[]{:S(2)}, u32[]{:S(2)}) collective-permute-start(s32[128,6]{1,0:T(8,128)S(1)} %bitcast.210), channel_id=1, source_target_pairs={{0,20},{20,0},{4,16},{16,4},{1,21},{21,1},{5,17},{17,5},{2,22},{22... | collective-permute-start | bytes 9224 | tf_op jit(solution)/shard_map/ppermute | solution.py:163
  5.5 13.3 %collective-permute-start = (s32[128,6]{1,0:T(8,128)S(1)}, s32[128,6]{1,0:T(8,128)S(1)}, u32[]{:S(2)}, u32[]{:S(2)}) collective-permute-start(s32[128,6]{1,0:T(8,128)S(1)} %bitcast.211), channel_id=1, source_target_pairs={{0,16},{16,0},{1,17},{17,1},{2,18},{18,2},{3,19},{19,3},{4,20},{20... | collective-permute-start | bytes 9224 | tf_op jit(solution)/shard_map/ppermute | solution.py:12
  6.8 16.2 %collective-permute-start.3 = (bf16[64,2048]{1,0:T(8,128)(2,1)S(1)}, bf16[64,2048]{1,0:T(8,128)(2,1)S(1)}, u32[]{:S(2)}, u32[]{:S(2)}) collective-permute-start(bf16[64,2048]{1,0:T(8,128)(2,1)S(1)} %get-tuple-element.16), channel_id=1, source_target_pairs={{0,4},{4,0},{1,5},{5,1},{2,6},{6,2},{3,7},{7,3},{8,12},{12,8},{9,1... | collective-permute-start | bytes 786440 | tf_op jit(solution)/shard_map/ppermute | solution.py:49
  10.7 12.5 %copy-start.1 = (f32[1,2048]{1,0:T(1,128)S(1)}, f32[1,2048]{1,0:T(1,128)}, u32[]{:S(2)}) copy-start(f32[1,2048]{1,0:T(1,128)} %param.10) | copy-start | bytes 24580
  11.5 11.7 %collective-permute-start.1 = (f32[2048,33]{0,1:T(8,128)S(1)}, f32[2048,33]{0,1:T(8,128)S(1)}, u32[]{:S(2)}, u32[]{:S(2)}) collective-permute-start(f32[2048,33]{0,1:T(8,128)S(1)} %pad_maximum_fusion.4), channel_id=1, source_target_pairs={{0,16},{16,0},{1,17},{17,1},{2,18},{18,2},{3,19},{19,3},{4,20},{20... | collective-permute-start | bytes 811016 | tf_op jit(solution)/shard_map/ppermute | solution.py:12
  11.6 49.6 %collective-permute-start.6 = (bf16[4,1024,768]{2,1,0:T(8,128)(2,1)}, bf16[4,1024,768]{2,1,0:T(8,128)(2,1)}, u32[]{:S(2)}, u32[]{:S(2)}) collective-permute-start(bf16[4,1024,768]{2,1,0:T(8,128)(2,1)} %bitcast.218), channel_id=1, source_target_pairs={{0,16},{16,0},{1,17},{17,1},{2,18},{18,2},{3,19},{19,3},{4,20},{20... | collective-permute-start | bytes 18874376 | tf_op jit(solution)/shard_map/ppermute | solution.py:12
  17.9 48.2 %collective-permute-start.7 = (bf16[4,1024,768]{2,1,0:T(8,128)(2,1)}, bf16[4,1024,768]{2,1,0:T(8,128)(2,1)}, u32[]{:S(2)}, u32[]{:S(2)}) collective-permute-start(bf16[4,1024,768]{2,1,0:T(8,128)(2,1)} %bitcast.223), channel_id=1, source_target_pairs={{0,16},{16,0},{1,17},{17,1},{2,18},{18,2},{3,19},{19,3},{4,20},{20... | collective-permute-start | bytes 18874376 | tf_op jit(solution)/shard_map/ppermute | solution.py:12
  23.2 1.4 copy-start.2
  27.4 33.2 %all-to-all-start = ((bf16[8,4,28,1024]{3,1,2,0:T(4,128)(2,1)}), bf16[8,4,28,1024]{3,1,2,0:T(4,128)(2,1)S(1)}, u32[]{:S(2)}, u32[]{:S(2)}) async-start(bf16[8,4,28,1024]{3,1,2,0:T(4,128)(2,1)} %bitcast.198), calls=%async_computation | async-start | bytes 3670016 | tf_op jit(solution)/shard_map/all_to_all | solution.py:97
  31.5 84.4 %collective-permute-start.2 = (bf16[4,768,1024]{2,1,0:T(8,128)(2,1)}, bf16[4,768,1024]{2,1,0:T(8,128)(2,1)}, u32[]{:S(2)}, u32[]{:S(2)}) collective-permute-start(bf16[4,768,1024]{2,1,0:T(8,128)(2,1)} %bitcast.228), channel_id=1, source_target_pairs={{0,16},{16,0},{1,17},{17,1},{2,18},{18,2},{3,19},{19,3},{4,20},{20... | collective-permute-start | bytes 18874376 | tf_op jit(solution)/shard_map/ppermute | solution.py:12
  60.6 5.5 %slice-start.4 = ((s8[6291456]{0:T(1024)(128)(4,1)}), s8[4194304]{0:T(1024)(128)(4,1)S(1)}, s32[]{:S(2)}) async-start(s8[6291456]{0:T(1024)(128)(4,1)} %bitcast.224), calls=%async_computation.9 | async-start | bytes 8388608
  61.2 4.9 %slice-start.5 = ((s8[6291456]{0:T(1024)(128)(4,1)}), s8[2097152]{0:T(1024)(128)(4,1)S(1)}, s32[]{:S(2)}) async-start(s8[6291456]{0:T(1024)(128)(4,1)} %bitcast.224), calls=%async_computation.10 | async-start | bytes 4194304
  61.2 37.5 %slice-start = ((s8[6291456]{0:T(1024)(128)(4,1)}), s8[4194304]{0:T(1024)(128)(4,1)S(1)}, s32[]{:S(2)}) async-start(s8[6291456]{0:T(1024)(128)(4,1)} %bitcast.219), calls=%async_computation.5 | async-start | bytes 8388608
  66.0 32.7 %slice-start.1 = ((s8[6291456]{0:T(1024)(128)(4,1)}), s8[2097152]{0:T(1024)(128)(4,1)S(1)}, s32[]{:S(2)}) async-start(s8[6291456]{0:T(1024)(128)(4,1)} %bitcast.219), calls=%async_computation.6 | async-start | bytes 4194304
  68.1 30.7 %collective-permute-start.8 = (bf16[2,4,112,768]{3,2,1,0:T(8,128)(2,1)S(1)}, bf16[2,4,112,768]{3,2,1,0:T(8,128)(2,1)S(1)}, u32[]{:S(2)}, u32[]{:S(2)}) collective-permute-start(bf16[2,4,112,768]{3,2,1,0:T(8,128)(2,1)S(1)} %pad_maximum_fusion), channel_id=1, source_target_pairs={{0,8},{8,0},{1,9},{9,1},{2,10},{10,2},{3,11},{11,3},{4,12},{12,4},... | collective-permute-start | bytes 4128776 | tf_op jit(solution)/shard_map/ppermute | solution.py:112
  102.7 11.5 %collective-permute-start.9 = (bf16[4,112,768]{2,1,0:T(8,128)(2,1)S(1)}, bf16[4,112,768]{2,1,0:T(8,128)(2,1)S(1)}, u32[]{:S(2)}, u32[]{:S(2)}) collective-permute-start(bf16[4,112,768]{2,1,0:T(8,128)(2,1)S(1)} %multiply_convert_fusion.1), channel_id=1, source_target_pairs={{0,8},{8,0},{1,9},{9,1},{2,10},{10,2},{3,11},{11,3},{4,12},{12,4},... | collective-permute-start | bytes 2064392 | tf_op jit(solution)/shard_map/ppermute | solution.py:122
  122.3 4.6 %copy-start = (bf16[1,2048,32]{1,2,0:T(8,128)(2,1)S(1)}, bf16[1,2048,32]{1,2,0:T(8,128)(2,1)}, u32[]{:S(2)}) copy-start(bf16[1,2048,32]{1,2,0:T(8,128)(2,1)} %param.11) | copy-start | bytes 393220
  122.3 4.6 %copy-start.3 = (f32[2048,33]{0,1:T(8,128)S(1)}, f32[2048,33]{0,1:T(8,128)}, u32[]{:S(2)}) copy-start(f32[2048,33]{0,1:T(8,128)} %copy-done.2) | copy-start | bytes 811012
  122.3 44.2 %all-to-all-start.1 = ((bf16[16,56,1024]{2,1,0:T(8,128)(2,1)}), bf16[16,56,1024]{2,1,0:T(8,128)(2,1)S(1)}, u32[]{:S(2)}, u32[]{:S(2)}) async-start(bf16[16,56,1024]{2,1,0:T(8,128)(2,1)} %reshape.228), calls=%async_computation.1 | async-start | bytes 3670016 | tf_op jit(solution)/shard_map/all_to_all | solution.py:130
  168.3 13.1 %collective-permute-start.10 = (bf16[64,2048]{1,0:T(8,128)(2,1)S(1)}, bf16[64,2048]{1,0:T(8,128)(2,1)S(1)}, u32[]{:S(2)}, u32[]{:S(2)}) collective-permute-start(bf16[64,2048]{1,0:T(8,128)(2,1)S(1)} %get-tuple-element.33), channel_id=1, source_target_pairs={{0,4},{4,0},{1,5},{5,1},{2,6},{6,2},{3,7},{7,3},{8,12},{12,8},{9,1... | collective-permute-start | bytes 786440 | tf_op jit(solution)/shard_map/ppermute | solution.py:49
  181.9 31.7 %slice-start.2 = ((s8[6291456]{0:T(1024)(128)(4,1)}), s8[2097152]{0:T(1024)(128)(4,1)S(1)}, s32[]{:S(2)}) async-start(s8[6291456]{0:T(1024)(128)(4,1)} %bitcast.221), calls=%async_computation.7 | async-start | bytes 4194304
  183.0 30.5 %slice-start.3 = ((s8[6291456]{0:T(1024)(128)(4,1)}), s8[4194304]{0:T(1024)(128)(4,1)S(1)}, s32[]{:S(2)}) async-start(s8[6291456]{0:T(1024)(128)(4,1)} %bitcast.221), calls=%async_computation.8 | async-start | bytes 8388608
  212.9 5.5 %slice-start.6 = ((s8[6291456]{0:T(1024)(128)(4,1)}), s8[4194304]{0:T(1024)(128)(4,1)S(1)}, s32[]{:S(2)}) async-start(s8[6291456]{0:T(1024)(128)(4,1)} %bitcast.226), calls=%async_computation.11 | async-start | bytes 8388608
  213.6 4.8 %slice-start.7 = ((s8[6291456]{0:T(1024)(128)(4,1)}), s8[2097152]{0:T(1024)(128)(4,1)S(1)}, s32[]{:S(2)}) async-start(s8[6291456]{0:T(1024)(128)(4,1)} %bitcast.226), calls=%async_computation.12 | async-start | bytes 4194304
  223.3 27.2 %collective-permute-start.11 = (bf16[2,4,112,768]{3,2,1,0:T(8,128)(2,1)S(1)}, bf16[2,4,112,768]{3,2,1,0:T(8,128)(2,1)S(1)}, u32[]{:S(2)}, u32[]{:S(2)}) collective-permute-start(bf16[2,4,112,768]{3,2,1,0:T(8,128)(2,1)S(1)} %pad_maximum_fusion.2), channel_id=1, source_target_pairs={{0,8},{8,0},{1,9},{9,1},{2,10},{10,2},{3,11},{11,3},{4,12},{12,4},... | collective-permute-start | bytes 4128776 | tf_op jit(solution)/shard_map/ppermute | solution.py:112
  260.2 11.0 %collective-permute-start.12 = (bf16[4,112,768]{2,1,0:T(8,128)(2,1)S(1)}, bf16[4,112,768]{2,1,0:T(8,128)(2,1)S(1)}, u32[]{:S(2)}, u32[]{:S(2)}) collective-permute-start(bf16[4,112,768]{2,1,0:T(8,128)(2,1)S(1)} %multiply_convert_fusion), channel_id=1, source_target_pairs={{0,8},{8,0},{1,9},{9,1},{2,10},{10,2},{3,11},{11,3},{4,12},{12,4},... | collective-permute-start | bytes 2064392 | tf_op jit(solution)/shard_map/ppermute | solution.py:122
  281.1 4.5 %copy-start.4 = (f32[2048,33]{0,1:T(8,128)S(1)}, f32[2048,33]{0,1:T(8,128)}, u32[]{:S(2)}) copy-start(f32[2048,33]{0,1:T(8,128)} %copy-done.2) | copy-start | bytes 811012
  281.1 32.7 %all-to-all-start.3 = ((bf16[16,56,1024]{2,1,0:T(8,128)(2,1)}), bf16[16,56,1024]{2,1,0:T(8,128)(2,1)S(1)}, u32[]{:S(2)}, u32[]{:S(2)}) async-start(bf16[16,56,1024]{2,1,0:T(8,128)(2,1)} %reshape.230), calls=%async_computation.3 | async-start | bytes 3670016 | tf_op jit(solution)/shard_map/all_to_all | solution.py:130
  317.6 10.2 %all-to-all-start.4 = ((f32[32,1,2]{2,1,0:T(1,128)}), f32[32,1,2]{2,1,0:T(1,128)S(1)}, u32[]{:S(2)}, u32[]{:S(2)}) async-start(f32[32,1,2]{2,1,0:T(1,128)} %broadcast_in_dim.32), calls=%async_computation.4 | async-start | bytes 32768 | tf_op jit(solution)/shard_map/all_to_all | solution.py:185
  320.7 7.7 %collective-permute-start.13 = (bf16[64,1024]{1,0:T(8,128)(2,1)S(1)}, bf16[64,1024]{1,0:T(8,128)(2,1)S(1)}, u32[]{:S(2)}, u32[]{:S(2)}) collective-permute-start(bf16[64,1024]{1,0:T(8,128)(2,1)S(1)} %get-tuple-element.28), channel_id=1, source_target_pairs={{0,16},{16,0},{1,17},{17,1},{2,18},{18,2},{3,19},{19,3},{4,20},{20... | collective-permute-start | bytes 393224 | tf_op jit(solution)/shard_map/ppermute | solution.py:12
where the time goes:
time: 330 us; the launch traced here: 329 us
  waiting for transfers between devices  199 us (60%)
  matrix products  47.2 us (14%)
  starting transfers between devices  28.7 us (9%)
  blocking collectives  28.3 us (9%)
  local copies, waits for them, and re-layouts  16.9 us (5%)
  other arithmetic  7.57 us (2%)
    all_to_all x2, waiting for transfers between devices, expert_layer(): lax.all_to_all(sending.reshape(sources, group_slots, chunk), ('fsdp', 'zh...  66.6 us
    ppermute x2, waiting for transfers between devices, expert_layer(): lax.ppermute(outgoing_pair, 'fsdp', ring_pairs(fsdp_count, shift))  56.6 us
    all_to_all x1, waiting for transfers between devices, expert_layer(): arrived = lax.all_to_all(outgoing, ('fsdp', 'inner'), 0, 2, tiled=True)  29 us
    all_to_all x1, blocking collectives, expert_layer(): arrived = lax.all_to_all(outgoing, ('fsdp', 'inner'), 0, 2, tiled=True)  28.3 us
    ppermute x2, waiting for transfers between devices, expert_layer(): lax.ppermute(inner_act, 'fsdp', ring_pairs(fsdp_count, shift))  21.2 us
    dot_general x4, matrix products, gate_and_up(): jnp.einsum('jrd,jdh->jrh', rows_in, gate_w, preferred_element_type=jnp.fl...  16.2 us
    dot_general x4, matrix products, gate_and_up(): jnp.einsum('jrd,jdh->jrh', rows_in, up_w, preferred_element_type=jnp.floa...  13.5 us
    ppermute x3, waiting for transfers between devices, other_half(): return lax.ppermute(value, 'zhalf', [(0, 1), (1, 0)])  13.3 us
  transfers between devices with their start and end apart: 18, of which 11 were waited for; matrix products, arithmetic and copies ran while one was open for 8% of the time, Pallas kernels for 0%

commit v1 on v0

--- a/solution.py
+++ b/solution.py
@@ -94,7 +94,15 @@
         .astype(jnp.bfloat16)
         .reshape(fsdp_count * inner_devices, local_experts, halves * capacity, chunk)
     )
-    arrived = lax.all_to_all(outgoing, ("fsdp", "inner"), 0, 2, tiled=True)
+    arrived = jnp.concatenate(
+        lax.all_to_all(
+            jnp.stack(jnp.split(outgoing, lax.axis_size(("fsdp", "inner")), 0), 0),
+            ("fsdp", "inner"),
+            0,
+            0,
+        ),
+        2,
+    )
     sources = fsdp_count * inner_devices * halves
     arrived_blocks = arrived.reshape(local_experts, fsdp_count, -1, chunk)
 

time: 330 us -> 343 us (1.039); the launches traced: 329 us -> 338 us
  local copies, waits for them, and re-layouts: 16.9 us -> 23.4 us
    ppermute x3, waiting for transfers between devices: 13.3 us -> 20.6 us  [other_half(): return lax.ppermute(value, 'zhalf', [(0, 1), (1, 0)])]
    unnamed x27 -> x41, local copies, waits for them, and re-layouts: 0.87 us -> 7.66 us
    ppermute x1, waiting for transfers between devices: 5.71 us -> 0.36 us  [body(): lax.ppermute(own_routes, ('section', 'zhalf'), [(0, 3), (3, 0), (1, 2), (...]
    ppermute x3, starting transfers between devices: 9 us -> 4.61 us  [other_half(): return lax.ppermute(value, 'zhalf', [(0, 1), (1, 0)])]
    ppermute x1, starting transfers between devices: 0.01 us -> 3.69 us  [body(): lax.ppermute(own_routes, ('section', 'zhalf'), [(0, 3), (3, 0), (1, 2), (...]
  transfers between devices with their start and end apart: 18 -> 18, of which waited for: 11 -> 12; matrix products, arithmetic and copies ran while one was open for 8% -> 9% of each run, Pallas kernels for 0% -> 0%
where the time goes in v1:
time: 343 us; the launch traced here: 338 us
  waiting for transfers between devices  200 us (58%)
  matrix products  47.5 us (14%)
  starting transfers between devices  29.2 us (9%)
  blocking collectives  28.2 us (8%)
  local copies, waits for them, and re-layouts  23.4 us (7%)
  other arithmetic  7.5 us (2%)
    all_to_all x2, waiting for transfers between devices, expert_layer(): lax.all_to_all(sending.reshape(sources, group_slots, chunk), ('fsdp', 'zh...  66.3 us
    ppermute x2, waiting for transfers between devices, expert_layer(): lax.ppermute(outgoing_pair, 'fsdp', ring_pairs(fsdp_count, shift))  56.9 us
    all_to_all x1, blocking collectives, expert_layer(): lax.all_to_all(jnp.stack(jnp.split(outgoing, lax.axis_size(('fsdp', 'inne...  28.2 us
    all_to_all x1, waiting for transfers between devices, expert_layer(): lax.all_to_all(jnp.stack(jnp.split(outgoing, lax.axis_size(('fsdp', 'inne...  27.8 us
    ppermute x2, waiting for transfers between devices, expert_layer(): lax.ppermute(inner_act, 'fsdp', ring_pairs(fsdp_count, shift))  21.5 us
    ppermute x3, waiting for transfers between devices, other_half(): return lax.ppermute(value, 'zhalf', [(0, 1), (1, 0)])  20.6 us
    dot_general x4, matrix products, gate_and_up(): jnp.einsum('jrd,jdh->jrh', rows_in, up_w, preferred_element_type=jnp.floa...  16.8 us
    dot_general x4, matrix products, gate_and_up(): jnp.einsum('jrd,jdh->jrh', rows_in, gate_w, preferred_element_type=jnp.fl...  13.2 us
  transfers between devices with their start and end apart: 18, of which 12 were waited for; matrix products, arithmetic and copies ran while one was open for 9% of the time, Pallas kernels for 0%

profile of v1, /device:TPU:0, one launch (start us, length us, event | category | flops | bytes accessed | tf_op | source)
XLA Modules:
  0.0 337.8 jit_solution(2989197542513364269)
XLA Ops:
  0.6 0.8 copy.121
  1.4 0.6 collective-permute-start
  2.0 3.7 %collective-permute-start.5 = (s32[128,6]{1,0:T(8,128)S(1)}, s32[128,6]{1,0:T(8,128)S(1)}, u32[]{:S(2)}, u32[]{:S(2)}) collective-permute-start(s32[128,6]{1,0:T(8,128)S(1)} %bitcast.284), channel_id=1, source_target_pairs={{0,20},{20,0},{4,16},{16,4},{1,21},{21,1},{5,17},{17,5},{2,22},{22... | collective-permute-start | bytes 9224 | tf_op jit(solution)/shard_map/ppermute | solution.py:171
  5.7 0.9 bitcast_convert_fusion
  6.6 0.7 pad_maximum_fusion.4
  7.9 1.1 fusion.78
  9.5 2.6 collective-permute-start.3
  15.3 9.2 %collective-permute-done.3 = bf16[64,2048]{1,0:T(8,128)(2,1)S(1)} collective-permute-done((bf16[64,2048]{1,0:T(8,128)(2,1)S(1)}, bf16[64,2048]{1,0:T(8,128)(2,1)S(1)}, u32[]{:S(2)}, u32[]{:S(2)}) %collective-permute-start.3) | collective-permute-done | bytes 262176 | tf_op jit(solution)/shard_map/ppermute | solution.py:49
  24.7 0.7 copy-done.2
  26.1 0.7 convert_bitcast_fusion.3
  26.8 1.6 copy.128
  28.4 0.8 fusion.104
  29.2 0.8 fusion.103
  29.9 0.8 fusion.102
  30.7 0.8 fusion.101
  31.5 0.8 fusion.100
  32.2 0.8 fusion.99
  33.0 0.8 fusion.98
  33.8 0.8 fusion.97
  34.5 4.0 %all-to-all-start = ((bf16[8,1,4,28,1024]{4,2,3,1,0:T(4,128)(2,1)}), bf16[8,1,4,28,1024]{4,2,3,1,0:T(4,128)(2,1)S(1)}, u32[]{:S(2)}, u32[]{:S(2)}) async-start(bf16[8,1,4,28,1024]{4,2,3,1,0:T(4,128)(2,1)} %fusion.97), calls=%async_computation | async-start | bytes 3670016 | tf_op jit(solution)/shard_map/all_to_all | solution.py:98
  38.6 27.8 %all-to-all-done = bf16[8,1,4,28,1024]{4,2,3,1,0:T(4,128)(2,1)S(1)} async-done(((bf16[8,1,4,28,1024]{4,2,3,1,0:T(4,128)(2,1)}), bf16[8,1,4,28,1024]{4,2,3,1,0:T(4,128)(2,1)S(1)}, u32[]{:S(2)}, u32[]{:S(2)}) %all-to-all-start) | async-done | bytes 1835040 | tf_op jit(solution)/shard_map/all_to_all | solution.py:98
  66.4 0.6 constant_dynamic-slice_fusion.4
  67.0 4.8 %fusion.33 = bf16[1,4,112,768]{3,2,1,0:T(8,128)(2,1)S(1)} fusion(bf16[4,1024,768]{2,1,0:T(8,128)(2,1)} %collective-permute-done.7, pred[]{:T(512)S(6)} %eq.78, bf16[4,1,112,1024]{3,0,2,1:T(4,128)(2,1)S(1)} %get-tuple-element.19, bf16[1,4,1024,768]{3,2,1,0:T(8,128)(2,1)} %param.13), kind=kOutput, calls=%fused_computation.49 | convolution fusion | flops 708132864 | bytes 14188545 | tf_op jit(solution)/shard_map/jrd,jdh->jrh/dot_general | solution.py:111
  71.9 1.8 fusion.32
  73.9 0.6 collective-permute-start.8
  74.5 30.5 %collective-permute-done.8 = bf16[2,4,112,768]{3,2,1,0:T(8,128)(2,1)S(1)} collective-permute-done((bf16[2,4,112,768]{3,2,1,0:T(8,128)(2,1)S(1)}, bf16[2,4,112,768]{3,2,1,0:T(8,128)(2,1)S(1)}, u32[]{:S(2)}, u32[]{:S(2)}) %collective-permute-start.8) | collective-permute-done | bytes 1376288 | tf_op jit(solution)/shard_map/ppermute | solution.py:120
  105.0 1.9 fusion.27
  106.9 2.0 multiply_convert_fusion.1
  109.0 0.6 collective-permute-start.9
  109.6 11.2 %collective-permute-done.9 = bf16[4,112,768]{2,1,0:T(8,128)(2,1)S(1)} collective-permute-done((bf16[4,112,768]{2,1,0:T(8,128)(2,1)S(1)}, bf16[4,112,768]{2,1,0:T(8,128)(2,1)S(1)}, u32[]{:S(2)}, u32[]{:S(2)}) %collective-permute-start.9) | collective-permute-done | bytes 688160 | tf_op jit(solution)/shard_map/ppermute | solution.py:130
  120.9 0.6 gather_fusion
  121.7 0.7 copy.131
  122.5 4.7 %convert_bitcast_fusion.2 = bf16[2,2,4,4,14,1024]{5,4,1,2,0,3:T(8,128)(2,1)S(1)} fusion(bf16[4,768,1024]{2,1,0:T(8,128)(2,1)} %collective-permute-done.2, pred[]{:T(512)S(6)} %eq.78, bf16[2,4,4,2,14,768]{5,1,4,3,2,0:T(4,128)(2,1)S(1)} %bitcast.277, bf16[1,4,768,1024]{3,2,1,0:T(8,128)(2,1)} %param.14), kind=kOutput, calls=%fused_computation.28 | convolution fusion | flops 1413349376 | bytes 15794177 | tf_op jit(solution)/shard_map/fjipch,jhd->fpijcd/dot_general | solution.py:135
  127.4 1.5 reshape.226
  128.9 5.4 %all-to-all-start.1 = ((bf16[16,56,1024]{2,1,0:T(8,128)(2,1)}), bf16[16,56,1024]{2,1,0:T(8,128)(2,1)S(1)}, u32[]{:S(2)}, u32[]{:S(2)}) async-start(bf16[16,56,1024]{2,1,0:T(8,128)(2,1)} %reshape.226), calls=%async_computation.1 | async-start | bytes 3670016 | tf_op jit(solution)/shard_map/all_to_all | solution.py:138
  135.0 39.0 %all-to-all-done.1 = bf16[16,56,1024]{2,1,0:T(8,128)(2,1)S(1)} async-done(((bf16[16,56,1024]{2,1,0:T(8,128)(2,1)}), bf16[16,56,1024]{2,1,0:T(8,128)(2,1)S(1)}, u32[]{:S(2)}, u32[]{:S(2)}) %all-to-all-start.1) | async-done | bytes 1835040 | tf_op jit(solution)/shard_map/all_to_all | solution.py:138
  174.1 1.7 fusion.70
  175.8 2.0 collective-permute-start.10
  178.0 10.9 %collective-permute-done.10 = bf16[64,2048]{1,0:T(8,128)(2,1)S(1)} collective-permute-done((bf16[64,2048]{1,0:T(8,128)(2,1)S(1)}, bf16[64,2048]{1,0:T(8,128)(2,1)S(1)}, u32[]{:S(2)}, u32[]{:S(2)}) %collective-permute-start.10) | collective-permute-done | bytes 262176 | tf_op jit(solution)/shard_map/ppermute | solution.py:49
  189.8 0.7 convert_bitcast_fusion.1
  190.5 1.6 copy.142
  192.9 28.2 %all_to_all.26 = bf16[8,1,4,28,1024]{4,2,3,1,0:T(4,128)(2,1)S(1)} all-to-all(bf16[8,1,4,28,1024]{4,2,3,1,0:T(4,128)(2,1)S(1)} %fusion.89), channel_id=1, replica_groups=mesh['section'=2,'fsdp'=2,'zhalf'=2,'inner'=4] {'fsdp','inner'}, dimensions={0} | all-to-all | bytes 3670016 | tf_op jit(solution)/shard_map/all_to_all | solution.py:98
  221.1 0.6 constant_dynamic-slice_fusion.2
  221.8 5.1 %fusion.35 = bf16[1,4,112,768]{3,2,1,0:T(8,128)(2,1)S(1)} fusion(bf16[4,1024,768]{2,1,0:T(8,128)(2,1)} %collective-permute-done.7, pred[]{:T(512)S(6)} %eq.172, bf16[4,1,112,1024]{3,0,2,1:T(4,128)(2,1)S(1)} %get-tuple-element.17, bf16[1,4,1024,768]{3,2,1,0:T(8,128)(2,1)S(1)} %bitcast.301), kind=kOutput, calls=%fused_computation.51 | convolution fusion | flops 708132864 | bytes 14188545 | tf_op jit(solution)/shard_map/jrd,jdh->jrh/dot_general | solution.py:111
  226.9 4.7 %fusion.34 = bf16[1,4,112,768]{3,2,1,0:T(8,128)(2,1)S(1)} fusion(bf16[4,1024,768]{2,1,0:T(8,128)(2,1)} %collective-permute-done.6, pred[]{:T(512)S(6)} %eq.172, bf16[4,1,112,1024]{3,0,2,1:T(4,128)(2,1)S(1)} %get-tuple-element.17, bf16[1,4,1024,768]{3,2,1,0:T(8,128)(2,1)S(1)} %bitcast.296), kind=kOutput, calls=%fused_computation.50 | convolution fusion | flops 708132864 | bytes 14188545 | tf_op jit(solution)/shard_map/jrd,jdh->jrh/dot_general | solution.py:110
  231.8 0.6 collective-permute-start.11
  232.4 26.4 %collective-permute-done.11 = bf16[2,4,112,768]{3,2,1,0:T(8,128)(2,1)S(1)} collective-permute-done((bf16[2,4,112,768]{3,2,1,0:T(8,128)(2,1)S(1)}, bf16[2,4,112,768]{3,2,1,0:T(8,128)(2,1)S(1)}, u32[]{:S(2)}, u32[]{:S(2)}) %collective-permute-start.11) | collective-permute-done | bytes 1376288 | tf_op jit(solution)/shard_map/ppermute | solution.py:120
  258.8 4.7 %fusion.25 = f32[4,112,768]{2,1,0:T(8,128)S(1)} fusion(bf16[4,1024,768]{2,1,0:T(8,128)(2,1)} %collective-permute-done.6, pred[]{:T(512)S(6)} %eq.172, bf16[4,1,112,1024]{3,0,2,1:T(4,128)(2,1)S(1)} %get-tuple-element.18, bf16[2,4,112,768]{3,2,1,0:T(8,128)(2,1)S(1)} %collective-permute-done.11, bf16[1,4,1024,768]{3,2,1,0:T(8,128)(2,1)S(1)} %bitcast.296), kind=kOutput, calls=%fused_computation.33 | convolution fusion | flops 708476928 | bytes 15564801 | tf_op jit(solution)/shard_map/jrd,jdh->jrh/dot_general | solution.py:110
  263.5 4.9 %multiply_convert_fusion = bf16[4,112,768]{2,1,0:T(8,128)(2,1)S(1)} fusion(f32[4,112,768]{2,1,0:T(8,128)S(1)} %fusion.25, bf16[4,1024,768]{2,1,0:T(8,128)(2,1)} %collective-permute-done.7, pred[]{:T(512)S(6)} %eq.172, bf16[4,1,112,1024]{3,0,2,1:T(4,128)(2,1)S(1)} %get-tuple-element.18, bf16[2,4,112,768]{3,2,1,0:T(8,128)(2,1)S(1)} %collective-permute-done.11, ...), kind=kOutput, calls=%fused_computation.40 | convolution fusion | flops 710541312 | bytes 16252929 | tf_op jit(solution)/shard_map/jrd,jdh->jrh/dot_general | solution.py:111
  268.5 0.6 collective-permute-start.12
  269.1 10.4 %collective-permute-done.12 = bf16[4,112,768]{2,1,0:T(8,128)(2,1)S(1)} collective-permute-done((bf16[4,112,768]{2,1,0:T(8,128)(2,1)S(1)}, bf16[4,112,768]{2,1,0:T(8,128)(2,1)S(1)}, u32[]{:S(2)}, u32[]{:S(2)}) %collective-permute-start.12) | collective-permute-done | bytes 688160 | tf_op jit(solution)/shard_map/ppermute | solution.py:130
  279.6 0.6 gather_fusion.1
  280.5 0.7 copy.145
  281.2 6.5 %convert_bitcast_fusion = bf16[2,2,4,4,14,1024]{5,4,1,2,0,3:T(8,128)(2,1)S(1)} fusion(bf16[4,768,1024]{2,1,0:T(8,128)(2,1)} %collective-permute-done.2, pred[]{:T(512)S(6)} %eq.172, bf16[2,4,4,2,14,768]{5,1,4,3,2,0:T(4,128)(2,1)S(1)} %bitcast.278, bf16[1,4,768,1024]{3,2,1,0:T(8,128)(2,1)} %param.14), kind=kOutput, calls=%fused_computation.26 | convolution fusion | flops 1413349376 | bytes 15794177 | tf_op jit(solution)/shard_map/fjipch,jhd->fpijcd/dot_general | solution.py:135
  287.9 1.5 reshape.228
  289.4 4.5 %all-to-all-start.3 = ((bf16[16,56,1024]{2,1,0:T(8,128)(2,1)}), bf16[16,56,1024]{2,1,0:T(8,128)(2,1)S(1)}, u32[]{:S(2)}, u32[]{:S(2)}) async-start(bf16[16,56,1024]{2,1,0:T(8,128)(2,1)} %reshape.228), calls=%async_computation.3 | async-start | bytes 3670016 | tf_op jit(solution)/shard_map/all_to_all | solution.py:138
  294.6 27.4 %all-to-all-done.3 = bf16[16,56,1024]{2,1,0:T(8,128)(2,1)S(1)} async-done(((bf16[16,56,1024]{2,1,0:T(8,128)(2,1)}), bf16[16,56,1024]{2,1,0:T(8,128)(2,1)S(1)}, u32[]{:S(2)}, u32[]{:S(2)}) %all-to-all-start.3) | async-done | bytes 1835040 | tf_op jit(solution)/shard_map/all_to_all | solution.py:138
  322.2 1.7 multiply_reduce_fusion
  323.9 1.4 pad_maximum_fusion.5
  325.2 0.6 broadcast_in_dim.32
  325.8 3.1 all-to-all-start.4
  329.3 6.7 %all-to-all-done.4 = f32[32,1,2]{2,1,0:T(1,128)S(1)} async-done(((f32[32,1,2]{2,1,0:T(1,128)}), f32[32,1,2]{2,1,0:T(1,128)S(1)}, u32[]{:S(2)}, u32[]{:S(2)}) %all-to-all-start.4) | async-done | bytes 288 | tf_op jit(solution)/shard_map/all_to_all | solution.py:193
  336.1 0.6 dynamic_slice.48
  336.7 0.8 maximum_select_fusion
  (123 shorter events, 10.4 us)
Async XLA Ops:
  1.4 11.6 %collective-permute-start = (s32[128,6]{1,0:T(8,128)S(1)}, s32[128,6]{1,0:T(8,128)S(1)}, u32[]{:S(2)}, u32[]{:S(2)}) collective-permute-start(s32[128,6]{1,0:T(8,128)S(1)} %bitcast.283), channel_id=1, source_target_pairs={{0,16},{16,0},{1,17},{17,1},{2,18},{18,2},{3,19},{19,3},{4,20},{20... | collective-permute-start | bytes 9224 | tf_op jit(solution)/shard_map/ppermute | solution.py:12
  2.0 7.5 %collective-permute-start.5 = (s32[128,6]{1,0:T(8,128)S(1)}, s32[128,6]{1,0:T(8,128)S(1)}, u32[]{:S(2)}, u32[]{:S(2)}) collective-permute-start(s32[128,6]{1,0:T(8,128)S(1)} %bitcast.284), channel_id=1, source_target_pairs={{0,20},{20,0},{4,16},{16,4},{1,21},{21,1},{5,17},{17,5},{2,22},{22... | collective-permute-start | bytes 9224 | tf_op jit(solution)/shard_map/ppermute | solution.py:171
  5.7 6.9 %collective-permute-start.4 = (s32[128,6]{1,0:T(8,128)S(1)}, s32[128,6]{1,0:T(8,128)S(1)}, u32[]{:S(2)}, u32[]{:S(2)}) collective-permute-start(s32[128,6]{1,0:T(8,128)S(1)} %bitcast.285), channel_id=1, source_target_pairs={{0,4},{4,0},{1,5},{5,1},{2,6},{6,2},{3,7},{7,3},{8,12},{12,8},{9,1... | collective-permute-start | bytes 9224 | tf_op jit(solution)/shard_map/ppermute | solution.py:49
  7.4 17.3 %copy-start.1 = (f32[1,2048]{1,0:T(1,128)S(1)}, f32[1,2048]{1,0:T(1,128)}, u32[]{:S(2)}) copy-start(f32[1,2048]{1,0:T(1,128)} %param.10) | copy-start | bytes 24580
  7.4 17.3 %collective-permute-start.1 = (f32[2048,33]{0,1:T(8,128)S(1)}, f32[2048,33]{0,1:T(8,128)S(1)}, u32[]{:S(2)}, u32[]{:S(2)}) collective-permute-start(f32[2048,33]{0,1:T(8,128)S(1)} %pad_maximum_fusion.4), channel_id=1, source_target_pairs={{0,16},{16,0},{1,17},{17,1},{2,18},{18,2},{3,19},{19,3},{4,20},{20... | collective-permute-start | bytes 811016 | tf_op jit(solution)/shard_map/ppermute | solution.py:12
  7.5 64.3 %collective-permute-start.6 = (bf16[4,1024,768]{2,1,0:T(8,128)(2,1)}, bf16[4,1024,768]{2,1,0:T(8,128)(2,1)}, u32[]{:S(2)}, u32[]{:S(2)}) collective-permute-start(bf16[4,1024,768]{2,1,0:T(8,128)(2,1)} %bitcast.292), channel_id=1, source_target_pairs={{0,16},{16,0},{1,17},{17,1},{2,18},{18,2},{3,19},{19,3},{4,20},{20... | collective-permute-start | bytes 18874376 | tf_op jit(solution)/shard_map/ppermute | solution.py:12
  9.5 15.1 %collective-permute-start.3 = (bf16[64,2048]{1,0:T(8,128)(2,1)S(1)}, bf16[64,2048]{1,0:T(8,128)(2,1)S(1)}, u32[]{:S(2)}, u32[]{:S(2)}) collective-permute-start(bf16[64,2048]{1,0:T(8,128)(2,1)S(1)} %get-tuple-element.16), channel_id=1, source_target_pairs={{0,4},{4,0},{1,5},{5,1},{2,6},{6,2},{3,7},{7,3},{8,12},{12,8},{9,1... | collective-permute-start | bytes 786440 | tf_op jit(solution)/shard_map/ppermute | solution.py:49
  12.5 54.5 %collective-permute-start.7 = (bf16[4,1024,768]{2,1,0:T(8,128)(2,1)}, bf16[4,1024,768]{2,1,0:T(8,128)(2,1)}, u32[]{:S(2)}, u32[]{:S(2)}) collective-permute-start(bf16[4,1024,768]{2,1,0:T(8,128)(2,1)} %bitcast.297), channel_id=1, source_target_pairs={{0,16},{16,0},{1,17},{17,1},{2,18},{18,2},{3,19},{19,3},{4,20},{20... | collective-permute-start | bytes 18874376 | tf_op jit(solution)/shard_map/ppermute | solution.py:12
  24.7 0.7 copy-start.2
  34.5 31.8 %all-to-all-start = ((bf16[8,1,4,28,1024]{4,2,3,1,0:T(4,128)(2,1)}), bf16[8,1,4,28,1024]{4,2,3,1,0:T(4,128)(2,1)S(1)}, u32[]{:S(2)}, u32[]{:S(2)}) async-start(bf16[8,1,4,28,1024]{4,2,3,1,0:T(4,128)(2,1)} %fusion.97), calls=%async_computation | async-start | bytes 3670016 | tf_op jit(solution)/shard_map/all_to_all | solution.py:98
  38.5 83.9 %collective-permute-start.2 = (bf16[4,768,1024]{2,1,0:T(8,128)(2,1)}, bf16[4,768,1024]{2,1,0:T(8,128)(2,1)}, u32[]{:S(2)}, u32[]{:S(2)}) collective-permute-start(bf16[4,768,1024]{2,1,0:T(8,128)(2,1)} %bitcast.302), channel_id=1, source_target_pairs={{0,16},{16,0},{1,17},{17,1},{2,18},{18,2},{3,19},{19,3},{4,20},{20... | collective-permute-start | bytes 18874376 | tf_op jit(solution)/shard_map/ppermute | solution.py:12
  66.4 5.5 %slice-start = ((s8[6291456]{0:T(1024)(128)(4,1)}), s8[4194304]{0:T(1024)(128)(4,1)S(1)}, s32[]{:S(2)}) async-start(s8[6291456]{0:T(1024)(128)(4,1)} %bitcast.293), calls=%async_computation.5 | async-start | bytes 8388608
  67.0 4.8 %slice-start.1 = ((s8[6291456]{0:T(1024)(128)(4,1)}), s8[2097152]{0:T(1024)(128)(4,1)S(1)}, s32[]{:S(2)}) async-start(s8[6291456]{0:T(1024)(128)(4,1)} %bitcast.293), calls=%async_computation.6 | async-start | bytes 4194304
  73.7 33.2 %slice-start.4 = ((s8[6291456]{0:T(1024)(128)(4,1)}), s8[4194304]{0:T(1024)(128)(4,1)S(1)}, s32[]{:S(2)}) async-start(s8[6291456]{0:T(1024)(128)(4,1)} %bitcast.298), calls=%async_computation.9 | async-start | bytes 8388608
  73.9 31.1 %collective-permute-start.8 = (bf16[2,4,112,768]{3,2,1,0:T(8,128)(2,1)S(1)}, bf16[2,4,112,768]{3,2,1,0:T(8,128)(2,1)S(1)}, u32[]{:S(2)}, u32[]{:S(2)}) collective-permute-start(bf16[2,4,112,768]{3,2,1,0:T(8,128)(2,1)S(1)} %pad_maximum_fusion), channel_id=1, source_target_pairs={{0,8},{8,0},{1,9},{9,1},{2,10},{10,2},{3,11},{11,3},{4,12},{12,4},... | collective-permute-start | bytes 4128776 | tf_op jit(solution)/shard_map/ppermute | solution.py:120
  105.0 1.9 slice-start.5
  109.0 11.8 %collective-permute-start.9 = (bf16[4,112,768]{2,1,0:T(8,128)(2,1)S(1)}, bf16[4,112,768]{2,1,0:T(8,128)(2,1)S(1)}, u32[]{:S(2)}, u32[]{:S(2)}) collective-permute-start(bf16[4,112,768]{2,1,0:T(8,128)(2,1)S(1)} %multiply_convert_fusion.1), channel_id=1, source_target_pairs={{0,8},{8,0},{1,9},{9,1},{2,10},{10,2},{3,11},{11,3},{4,12},{12,4},... | collective-permute-start | bytes 2064392 | tf_op jit(solution)/shard_map/ppermute | solution.py:130
  128.9 5.5 %copy-start = (bf16[1,2048,32]{1,2,0:T(8,128)(2,1)S(1)}, bf16[1,2048,32]{1,2,0:T(8,128)(2,1)}, u32[]{:S(2)}) copy-start(bf16[1,2048,32]{1,2,0:T(8,128)(2,1)} %param.11) | copy-start | bytes 393220
  128.9 5.5 %copy-start.3 = (f32[2048,33]{0,1:T(8,128)S(1)}, f32[2048,33]{0,1:T(8,128)}, u32[]{:S(2)}) copy-start(f32[2048,33]{0,1:T(8,128)} %copy-done.2) | copy-start | bytes 811012
  128.9 45.1 %all-to-all-start.1 = ((bf16[16,56,1024]{2,1,0:T(8,128)(2,1)}), bf16[16,56,1024]{2,1,0:T(8,128)(2,1)S(1)}, u32[]{:S(2)}, u32[]{:S(2)}) async-start(bf16[16,56,1024]{2,1,0:T(8,128)(2,1)} %reshape.226), calls=%async_computation.1 | async-start | bytes 3670016 | tf_op jit(solution)/shard_map/all_to_all | solution.py:138
  175.8 13.1 %collective-permute-start.10 = (bf16[64,2048]{1,0:T(8,128)(2,1)S(1)}, bf16[64,2048]{1,0:T(8,128)(2,1)S(1)}, u32[]{:S(2)}, u32[]{:S(2)}) collective-permute-start(bf16[64,2048]{1,0:T(8,128)(2,1)S(1)} %get-tuple-element.33), channel_id=1, source_target_pairs={{0,4},{4,0},{1,5},{5,1},{2,6},{6,2},{3,7},{7,3},{8,12},{12,8},{9,1... | collective-permute-start | bytes 786440 | tf_op jit(solution)/shard_map/ppermute | solution.py:49
  190.5 31.2 %slice-start.6 = ((s8[6291456]{0:T(1024)(128)(4,1)}), s8[4194304]{0:T(1024)(128)(4,1)S(1)}, s32[]{:S(2)}) async-start(s8[6291456]{0:T(1024)(128)(4,1)} %bitcast.300), calls=%async_computation.11 | async-start | bytes 8388608
  192.8 29.0 %slice-start.7 = ((s8[6291456]{0:T(1024)(128)(4,1)}), s8[2097152]{0:T(1024)(128)(4,1)S(1)}, s32[]{:S(2)}) async-start(s8[6291456]{0:T(1024)(128)(4,1)} %bitcast.300), calls=%async_computation.12 | async-start | bytes 4194304
  221.1 5.8 %slice-start.2 = ((s8[6291456]{0:T(1024)(128)(4,1)}), s8[4194304]{0:T(1024)(128)(4,1)S(1)}, s32[]{:S(2)}) async-start(s8[6291456]{0:T(1024)(128)(4,1)} %bitcast.295), calls=%async_computation.7 | async-start | bytes 8388608
  221.8 5.1 %slice-start.3 = ((s8[6291456]{0:T(1024)(128)(4,1)}), s8[2097152]{0:T(1024)(128)(4,1)S(1)}, s32[]{:S(2)}) async-start(s8[6291456]{0:T(1024)(128)(4,1)} %bitcast.295), calls=%async_computation.8 | async-start | bytes 4194304
  231.8 27.0 %collective-permute-start.11 = (bf16[2,4,112,768]{3,2,1,0:T(8,128)(2,1)S(1)}, bf16[2,4,112,768]{3,2,1,0:T(8,128)(2,1)S(1)}, u32[]{:S(2)}, u32[]{:S(2)}) collective-permute-start(bf16[2,4,112,768]{3,2,1,0:T(8,128)(2,1)S(1)} %pad_maximum_fusion.2), channel_id=1, source_target_pairs={{0,8},{8,0},{1,9},{9,1},{2,10},{10,2},{3,11},{11,3},{4,12},{12,4},... | collective-permute-start | bytes 4128776 | tf_op jit(solution)/shard_map/ppermute | solution.py:120
  268.5 11.0 %collective-permute-start.12 = (bf16[4,112,768]{2,1,0:T(8,128)(2,1)S(1)}, bf16[4,112,768]{2,1,0:T(8,128)(2,1)S(1)}, u32[]{:S(2)}, u32[]{:S(2)}) collective-permute-start(bf16[4,112,768]{2,1,0:T(8,128)(2,1)S(1)} %multiply_convert_fusion), channel_id=1, source_target_pairs={{0,8},{8,0},{1,9},{9,1},{2,10},{10,2},{3,11},{11,3},{4,12},{12,4},... | collective-permute-start | bytes 2064392 | tf_op jit(solution)/shard_map/ppermute | solution.py:130
  289.4 4.6 %copy-start.4 = (f32[2048,33]{0,1:T(8,128)S(1)}, f32[2048,33]{0,1:T(8,128)}, u32[]{:S(2)}) copy-start(f32[2048,33]{0,1:T(8,128)} %copy-done.2) | copy-start | bytes 811012
  289.4 32.6 %all-to-all-start.3 = ((bf16[16,56,1024]{2,1,0:T(8,128)(2,1)}), bf16[16,56,1024]{2,1,0:T(8,128)(2,1)S(1)}, u32[]{:S(2)}, u32[]{:S(2)}) async-start(bf16[16,56,1024]{2,1,0:T(8,128)(2,1)} %reshape.228), calls=%async_computation.3 | async-start | bytes 3670016 | tf_op jit(solution)/shard_map/all_to_all | solution.py:138
  325.8 10.2 %all-to-all-start.4 = ((f32[32,1,2]{2,1,0:T(1,128)}), f32[32,1,2]{2,1,0:T(1,128)S(1)}, u32[]{:S(2)}, u32[]{:S(2)}) async-start(f32[32,1,2]{2,1,0:T(1,128)} %broadcast_in_dim.32), calls=%async_computation.4 | async-start | bytes 32768 | tf_op jit(solution)/shard_map/all_to_all | solution.py:193
  329.0 7.7 %collective-permute-start.13 = (bf16[64,1024]{1,0:T(8,128)(2,1)S(1)}, bf16[64,1024]{1,0:T(8,128)(2,1)S(1)}, u32[]{:S(2)}, u32[]{:S(2)}) collective-permute-start(bf16[64,1024]{1,0:T(8,128)(2,1)S(1)} %get-tuple-element.28), channel_id=1, source_target_pairs={{0,16},{16,0},{1,17},{17,1},{2,18},{18,2},{3,19},{19,3},{4,20},{20... | collective-permute-start | bytes 393224 | tf_op jit(solution)/shard_map/ppermute | solution.py:12
